TPU v7x, 256 devices: a whole 4x4x8 slice. The times are simulated.
256 devices in a mesh: tile: 16 (over y, z_hi), spec: 16 (over x, z_lo, core).
Axes of the slice: x: 4, y: 4, z: 8 (z_hi: 4, z_lo: 2; z = z_hi * 2 + z_lo), core: 2. Of those that a mesh axis runs over, the one named last changes fastest.
Arguments:
- latent: bfloat16 [32, 4096, 1024], P(None, ('tile', 'spec')), may hold values from -6 to 6
- basis: bfloat16 [224, 32], replicated, may hold values from -1 to 1
- response: bfloat16 [8, 224], replicated, may hold values from -0.375 to 0.375
- hyper_obs: bfloat16 [224, 1024, 256], P('spec', 'tile'), may hold values from -6 to 6
- multi_obs: bfloat16 [8, 4096, 1024], P(None, ('tile', 'spec')), may hold values from -6 to 6
Outputs:
- z_next: bfloat16 [32, 4096, 1024], P(None, ('tile', 'spec'))
- hs_residual: bfloat16 [224, 1024, 256], P('spec', 'tile')
All inputs are finite; a program needn't handle non-finite values.
Results may differ from a plain program's by a relative error of at most 0.0054.
Values may be sent and summed in bfloat16 or wider, within the bound.
No kernel may reach another device: no remote copies, remote signals or barrier semaphores. Data moves between devices by JAX's collectives and lax.ppermute only.
A program may use at most 128 MiB of HBM per device.

v0:
```python
import jax
import jax.numpy as jnp
from jax import lax
from jax.sharding import PartitionSpec as P

DECIM = 4
HALO = 128
step_size = 0.3


def with_halo(cells, sides, width):
    for axis, dim in sides:
        count = lax.axis_size(axis)
        ends = count - 1
        head = lax.slice_in_dim(cells, 0, width, axis=dim)
        tail = lax.slice_in_dim(cells, cells.shape[dim] - width, cells.shape[dim], axis=dim)
        cells = jnp.concatenate(
            [
                lax.ppermute(tail, axis, [(i, (i + 1) % count) for i in range(ends)]),
                cells,
                lax.ppermute(head, axis, [((i + 1) % count, i) for i in range(ends)]),
            ],
            axis=dim,
        )
    return cells


def profile(where_at):
    narrow = DECIM / 2.0
    decay_len = 3.0 * HALO / 8.0
    ripple = jnp.cos(where_at * (jnp.pi / 7.0))
    return (
        jnp.exp(-where_at * where_at / (2.0 * narrow * narrow))
        + 0.5 * jnp.exp(-jnp.abs(where_at) / decay_len) * ripple * ripple
    )


def kernel_values(offsets):
    every_offset = jnp.arange(-HALO, HALO + 1).astype(jnp.float32)
    energy = jnp.sqrt(jnp.sum(profile(every_offset) ** 2))
    inside = jnp.abs(offsets) <= HALO
    return jnp.where(inside, profile(offsets.astype(jnp.float32)) / energy, 0.0).astype(
        jnp.bfloat16
    )


def banded(count, width, stride, shift):
    period = width + stride * count
    at = jnp.arange(period)
    offsets = jnp.where(at < width, at, at - period) + shift
    period_values = kernel_values(offsets)
    rows = jnp.tile(period_values, count)[: count * (period - stride)]
    return rows.reshape(count, period - stride)[:, :width]


def split_dot(spec, wide, narrow):
    high_wide = lax.reduce_precision(wide, exponent_bits=8, mantissa_bits=7)
    high = high_wide.astype(jnp.bfloat16)
    low = (wide - high_wide).astype(jnp.bfloat16)
    f32 = jnp.float32
    return jnp.einsum(spec, high, narrow, preferred_element_type=f32) + jnp.einsum(
        spec, low, narrow, preferred_element_type=f32
    )


def shards(latent, basis, response, hyper_obs, multi_obs):
    highest = lax.Precision.HIGHEST
    f32 = jnp.float32
    bf16 = jnp.bfloat16
    n_spec = lax.axis_size("spec")
    n_tile = lax.axis_size("tile")
    tile_index = lax.axis_index("tile")
    group, coarse_rows, coarse_cols = hyper_obs.shape
    rows_dev = coarse_rows * DECIM
    rim = HALO // DECIM
    subspace, rows_here, width_cols = latent.shape
    chunk = coarse_cols // n_spec
    wide_rows = coarse_rows + 2 * rim
    basis_wide = basis.astype(f32)
    column_t = banded(coarse_cols, width_cols, DECIM, 0)
    own_rows = banded(wide_rows, rows_dev, DECIM, HALO)
    cols_done = jnp.einsum(
        "qrc,sjc->sqjr",
        latent,
        column_t.reshape(n_spec, chunk, width_cols),
        preferred_element_type=f32,
    ).astype(bf16)
    tile_rows = lax.all_to_all(cols_done, "spec", split_axis=0, concat_axis=3, tiled=True)[0]
    obs_split = hyper_obs.reshape(group, coarse_rows, n_spec, chunk).transpose(2, 0, 3, 1)
    obs_cols = lax.all_to_all(obs_split, "spec", split_axis=0, concat_axis=1, tiled=True)[0]
    resp_basis = jnp.dot(response.astype(f32), basis_wide, precision=highest)
    multi_pred = jnp.einsum("mq,qrc->mrc", resp_basis, latent.astype(f32), precision=highest)
    multi_resid = (multi_pred - multi_obs.astype(f32)).astype(bf16)
    multi_resid, obs_cols = lax.optimization_barrier((multi_resid, obs_cols))
    obs_proj = jnp.einsum("bq,bji->qji", basis, obs_cols, preferred_element_type=f32)
    own_part = jnp.einsum("qjr,er->qje", tile_rows, own_rows, preferred_element_type=f32)
    half = wide_rows // 2
    ends = n_tile - 1
    to_next = jnp.concatenate(
        [
            lax.slice_in_dim(own_part, half, wide_rows, axis=2),
            lax.slice_in_dim(obs_proj, coarse_rows - rim, coarse_rows, axis=2),
        ],
        axis=2,
    )
    to_prev = jnp.concatenate(
        [lax.slice_in_dim(own_part, 0, half, axis=2), lax.slice_in_dim(obs_proj, 0, rim, axis=2)],
        axis=2,
    )
    got_prev = lax.ppermute(to_next, "tile", [(i, i + 1) for i in range(ends)])
    got_next = lax.ppermute(to_prev, "tile", [(i + 1, i) for i in range(ends)])
    coef_blurred = own_part + jnp.concatenate(
        [lax.slice_in_dim(got_prev, 0, half, axis=2), lax.slice_in_dim(got_next, 0, half, axis=2)],
        axis=2,
    )
    coef_own = lax.slice_in_dim(coef_blurred, rim, rim + coarse_rows, axis=2)
    blurred = split_dot("qji,bq->bji", coef_own, basis)
    resid_cols = (blurred - obs_cols.astype(f32)).astype(bf16)
    coef_resid = jnp.einsum("bq,bji->qji", basis, resid_cols, preferred_element_type=f32)
    gram = jnp.einsum("bq,bp->qp", basis, basis, preferred_element_type=f32)
    coef_rim = jnp.concatenate(
        [
            lax.slice_in_dim(coef_blurred, 0, rim, axis=2),
            lax.slice_in_dim(coef_blurred, wide_rows - rim, wide_rows, axis=2),
        ],
        axis=2,
    )
    proj_rim = jnp.concatenate(
        [
            lax.slice_in_dim(got_prev, half, half + rim, axis=2),
            lax.slice_in_dim(got_next, half, half + rim, axis=2),
        ],
        axis=2,
    )
    resid_rim = jnp.einsum("qp,pji->qji", gram, coef_rim, precision=highest) - proj_rim
    rim_prev = jnp.where(tile_index > 0, lax.slice_in_dim(resid_rim, 0, rim, axis=2), 0.0)
    rim_next = jnp.where(tile_index < ends, lax.slice_in_dim(resid_rim, rim, 2 * rim, axis=2), 0.0)
    coef_wide = jnp.concatenate([rim_prev, coef_resid, rim_next], axis=2)
    back_split = split_dot(
        "qjk,ksr->sqrj", coef_wide, own_rows.reshape(wide_rows, n_spec, rows_here)
    ).astype(bf16)
    rows_pixel = lax.all_to_all(back_split, "spec", split_axis=0, concat_axis=3, tiled=True)[0]
    grad_hs = jnp.einsum("qrj,jc->qrc", rows_pixel, column_t, preferred_element_type=f32)
    resid_split = resid_cols.reshape(n_spec, group, chunk, coarse_rows)
    resid_split, _ = lax.optimization_barrier((resid_split, rows_pixel))
    resid_bands = lax.all_to_all(resid_split, "spec", split_axis=0, concat_axis=2, tiled=True)[0]
    hs_residual = resid_bands.transpose(0, 2, 1)
    grad_ms = jnp.einsum("mq,mrc->qrc", resp_basis, multi_resid.astype(f32), precision=highest)
    gradient = grad_hs + grad_ms
    z_next = (latent.astype(f32) - step_size * gradient).astype(bf16)
    return (z_next, hs_residual)


def solution(mesh):
    in_specs = (
        P(None, ("tile", "spec"), None),
        P(),
        P(),
        P("spec", "tile", None),
        P(None, ("tile", "spec"), None),
    )
    out_specs = (P(None, ("tile", "spec"), None), P("spec", "tile", None))
    return jax.shard_map(shards, mesh=mesh, in_specs=in_specs, out_specs=out_specs, check_vma=False)
```

profile of v0, /device:TPU:24, one launch (start us, length us, event | category | flops | bytes accessed | tf_op | source)
XLA Modules:
  0.0 100.2 jit_solution(10661442841546105906)
XLA Ops:
  0.6 0.7 fusion.49
  2.0 0.2 broadcast_bitcast_fusion
  2.3 0.2 copy.68
  2.6 1.7 %reshape.88 = bf16[256,2044]{1,0:T(8,128)(2,1)S(1)} reshape(bf16[523264]{0:T(1024)(128)(2,1)S(1)} %slice.70) | data formatting | bytes 2093056 | tf_op jit(solution)/shard_map/reshape | solution.py:53
  4.3 1.4 %fusion.55 = bf16[16,16,16,32]{3,2,1,0:T(8,128)(2,1)S(1)} fusion(bf16[16,16,1024,1]{2,1,3,0:T(8,128)(2,1)S(1)} %bitcast.123, bf16[32,16,1024]{2,1,0:T(8,128)(2,1)S(1)} %copy-done.1), kind=kOutput, calls=%fused_computation.85 | convolution fusion | flops 268566528 | bytes 1835008 | tf_op jit(solution)/shard_map/qrc,sjc->sqjr/dot_general | solution.py:82
  5.8 1.7 %reshape.104 = bf16[16,2,4096]{2,1,0:T(2,128)(2,1)} reshape(bf16[16,16,16,32]{3,2,1,0:T(8,128)(2,1)S(1)} %fusion.55) | data formatting | bytes 524288
  7.4 5.8 %all-to-all-start = ((bf16[16,2,4096]{2,1,0:T(2,128)(2,1)}), bf16[16,2,4096]{2,1,0:T(2,128)(2,1)S(1)}, u32[]{:S(2)}, u32[]{:S(2)}) async-start(bf16[16,2,4096]{2,1,0:T(2,128)(2,1)} %reshape.104), calls=%async_computation | async-start | bytes 524288 | tf_op jit(solution)/shard_map/all_to_all | solution.py:88
  13.3 0.2 tile.9
  13.5 0.5 reshape.86
  14.0 1.5 %copy.50 = bf16[14,64,256]{1,2,0:T(8,128)(2,1)S(1)} copy(bf16[14,64,256]{2,1,0:T(8,128)(2,1)} %param.8) | data formatting | bytes 917504 | tf_op args[3]
  15.7 1.3 %reshape.102 = bf16[16,2,7168]{2,1,0:T(2,128)(2,1)} reshape(bf16[16,14,16,64]{3,2,1,0:T(8,128)(2,1)S(1)} %copy.51) | data formatting | bytes 917504
  17.0 4.3 %all-to-all-done = bf16[16,2,4096]{2,1,0:T(2,128)(2,1)S(1)} async-done(((bf16[16,2,4096]{2,1,0:T(2,128)(2,1)}), bf16[16,2,4096]{2,1,0:T(2,128)(2,1)S(1)}, u32[]{:S(2)}, u32[]{:S(2)}) %all-to-all-start) | async-done | bytes 262176 | tf_op jit(solution)/shard_map/all_to_all | solution.py:88
  21.3 3.6 %all-to-all-start.1 = ((bf16[16,2,7168]{2,1,0:T(2,128)(2,1)}), bf16[16,2,7168]{2,1,0:T(2,128)(2,1)S(1)}, u32[]{:S(2)}, u32[]{:S(2)}) async-start(bf16[16,2,7168]{2,1,0:T(2,128)(2,1)} %reshape.102), calls=%async_computation.1 | async-start | bytes 917504 | tf_op jit(solution)/shard_map/all_to_all | solution.py:90
  25.0 3.2 %fusion.8 = bf16[8,16,1024]{2,0,1:T(8,128)(2,1)} fusion(f32[8,32,1]{1,0,2:T(8,128)S(1)} %convolution_bitcast_fusion.2, bf16[32,16,1024]{2,1,0:T(8,128)(2,1)S(1)} %copy-done.1, bf16[8,16,1024]{2,1,0:T(8,128)(2,1)} %param.9), kind=kOutput, calls=%fused_computation.13 | convolution fusion | flops 50724864 | bytes 1573888 | tf_op jit(solution)/shard_map/mq,qrc->mrc/dot_general | solution.py:92
  28.2 0.5 reshape.105
  28.7 1.1 %copy.47 = bf16[32,16,256]{2,1,0:T(8,128)(2,1)S(1)} copy(bf16[32,16,256]{0,1,2:T(8,128)(2,1)S(1)} %bitcast.110) | data formatting | bytes 524288 | tf_op jit(solution)/shard_map/squeeze | solution.py:88
  29.8 0.2 fusion.25
  30.0 0.8 fusion.53
  30.8 4.1 %all-to-all-done.1 = bf16[16,2,7168]{2,1,0:T(2,128)(2,1)S(1)} async-done(((bf16[16,2,7168]{2,1,0:T(2,128)(2,1)}), bf16[16,2,7168]{2,1,0:T(2,128)(2,1)S(1)}, u32[]{:S(2)}, u32[]{:S(2)}) %all-to-all-start.1) | async-done | bytes 458784 | tf_op jit(solution)/shard_map/all_to_all | solution.py:90
  35.0 0.5 reshape.103
  35.5 0.7 copy.52
  36.3 0.3 fusion.30
  36.6 0.2 copy.93
  37.1 7.5 %collective-permute-start.1 = (f32[32,16,96]{2,1,0:T(8,128)S(1)}, f32[32,16,96]{2,1,0:T(8,128)S(1)}, u32[]{:S(2)}, u32[]{:S(2)}) collective-permute-start(f32[32,16,96]{2,1,0:T(8,128)S(1)} %pad_maximum_fusion.1), channel_id=1, source_target_pairs={{16,0},{32,16},{48,32},{64,48},{80,64},{96,80},{112,96},{128,112},... | collective-permute-start | bytes 589832 | tf_op jit(solution)/shard_map/ppermute | solution.py:111
  44.7 2.1 %collective-permute-start = (f32[32,16,96]{2,1,0:T(8,128)S(1)}, f32[32,16,96]{2,1,0:T(8,128)S(1)}, u32[]{:S(2)}, u32[]{:S(2)}) collective-permute-start(f32[32,16,96]{2,1,0:T(8,128)S(1)} %pad_maximum_fusion), channel_id=1, source_target_pairs={{0,16},{16,32},{32,48},{48,64},{64,80},{80,96},{96,112},{112,128},... | collective-permute-start | bytes 589832 | tf_op jit(solution)/shard_map/ppermute | solution.py:110
  47.1 8.2 %collective-permute-done.1 = f32[32,16,96]{2,1,0:T(8,128)S(1)} collective-permute-done((f32[32,16,96]{2,1,0:T(8,128)S(1)}, f32[32,16,96]{2,1,0:T(8,128)S(1)}, u32[]{:S(2)}, u32[]{:S(2)}) %collective-permute-start.1) | collective-permute-done | bytes 196640 | tf_op jit(solution)/shard_map/ppermute | solution.py:111
  55.3 7.2 %collective-permute-done = f32[32,16,96]{2,1,0:T(8,128)S(1)} collective-permute-done((f32[32,16,96]{2,1,0:T(8,128)S(1)}, f32[32,16,96]{2,1,0:T(8,128)S(1)}, u32[]{:S(2)}, u32[]{:S(2)}) %collective-permute-start) | collective-permute-done | bytes 196640 | tf_op jit(solution)/shard_map/ppermute | solution.py:110
  63.1 0.4 fusion.15
  63.8 0.2 maximum_subtract_fusion
  64.3 0.3 fusion.23
  64.7 0.3 fusion.7
  65.0 0.3 convolution_bitcast_fusion
  65.4 0.5 fusion.20
  65.9 0.5 fusion.58
  66.5 1.7 %reshape.106 = bf16[16,2,4096]{2,1,0:T(2,128)(2,1)} reshape(bf16[16,16,16,32]{3,2,1,0:T(8,128)(2,1)S(1)} %fusion.58) | data formatting | bytes 524288
  68.1 3.5 %all-to-all-start.2 = ((bf16[16,2,4096]{2,1,0:T(2,128)(2,1)}), bf16[16,2,4096]{2,1,0:T(2,128)(2,1)S(1)}, u32[]{:S(2)}, u32[]{:S(2)}) async-start(bf16[16,2,4096]{2,1,0:T(2,128)(2,1)} %reshape.106), calls=%async_computation.2 | async-start | bytes 524288 | tf_op jit(solution)/shard_map/all_to_all | solution.py:142
  71.7 0.8 copy.63
  72.5 7.2 %all-to-all-done.2 = bf16[16,2,4096]{2,1,0:T(2,128)(2,1)S(1)} async-done(((bf16[16,2,4096]{2,1,0:T(2,128)(2,1)}), bf16[16,2,4096]{2,1,0:T(2,128)(2,1)S(1)}, u32[]{:S(2)}, u32[]{:S(2)}) %all-to-all-start.2) | async-done | bytes 262176 | tf_op jit(solution)/shard_map/all_to_all | solution.py:142
  79.7 1.5 %reshape.107 = bf16[16,16,16,32]{3,2,1,0:T(8,128)(2,1)} reshape(bf16[16,2,4096]{2,1,0:T(2,128)(2,1)S(1)} %all-to-all-done.2) | data formatting | bytes 524288
  81.2 1.3 %reshape.108 = bf16[16,2,7168]{2,1,0:T(2,128)(2,1)} reshape(bf16[16,14,16,64]{3,2,1,0:T(8,128)(2,1)S(1)} %bitcast.115) | data formatting | bytes 917504
  82.4 4.2 %all-to-all-start.3 = ((bf16[16,2,7168]{2,1,0:T(2,128)(2,1)}), bf16[16,2,7168]{2,1,0:T(2,128)(2,1)}, u32[]{:S(2)}, u32[]{:S(2)}) async-start(bf16[16,2,7168]{2,1,0:T(2,128)(2,1)} %reshape.108), calls=%async_computation.3 | async-start | bytes 917504 | tf_op jit(solution)/shard_map/all_to_all | solution.py:146
  86.7 1.0 %fusion.61 = f32[32,16,1024]{2,0,1:T(8,128)S(1)} fusion(f32[8,32,1]{1,0,2:T(8,128)S(1)} %copy-done.7, bf16[8,16,1024]{2,0,1:T(8,128)(2,1)S(1)} %copy-done.3), kind=kOutput, calls=%fused_computation.87 | convolution fusion | flops 50331648 | bytes 2360320 | tf_op jit(solution)/shard_map/mq,mrc->qrc/dot_general | solution.py:148
  87.7 2.4 %copy.61 = bf16[32,16,256]{2,1,0:T(8,128)(2,1)S(1)} copy(bf16[32,16,256]{0,1,2:T(8,128)(2,1)} %bitcast.109) | data formatting | bytes 524288 | tf_op jit(solution)/shard_map/squeeze | solution.py:142
  90.1 3.4 %fusion.2 = bf16[32,16,1024]{2,1,0:T(8,128)(2,1)} fusion(f32[32,16,1024]{2,0,1:T(8,128)S(1)} %fusion.61, bf16[32,16,1024]{2,1,0:T(8,128)(2,1)S(1)} %copy-done.1, bf16[32,16,256]{2,1,0:T(8,128)(2,1)S(1)} %copy.61, bf16[256,2044]{1,0:T(8,128)(2,1)} %copy-done.2), kind=kOutput, calls=%fused_computation.3 | convolution fusion | flops 271056896 | bytes 4980736 | tf_op jit(solution)/shard_map/qrj,jc->qrc/dot_general | solution.py:143
  93.6 3.3 %all-to-all-done.3 = bf16[16,2,7168]{2,1,0:T(2,128)(2,1)} async-done(((bf16[16,2,7168]{2,1,0:T(2,128)(2,1)}), bf16[16,2,7168]{2,1,0:T(2,128)(2,1)}, u32[]{:S(2)}, u32[]{:S(2)}) %all-to-all-start.3) | async-done | bytes 458784 | tf_op jit(solution)/shard_map/all_to_all | solution.py:146
  96.8 2.1 %reshape.109 = bf16[16,14,16,64]{3,2,1,0:T(8,128)(2,1)S(1)} reshape(bf16[16,2,7168]{2,1,0:T(2,128)(2,1)} %all-to-all-done.3) | data formatting | bytes 917504
  98.9 0.2 copy.64
  99.2 1.1 %copy.65 = bf16[14,64,256]{2,1,0:T(8,128)(2,1)} copy(bf16[14,64,256]{1,2,0:T(8,128)(2,1)S(1)} %bitcast.113) | data formatting | bytes 917504
  (41 shorter events, 2.3 us)
Async XLA Ops:
  0.6 24.2 %copy-start = (bf16[224,32]{0,1:T(8,128)(2,1)S(1)}, bf16[224,32]{0,1:T(8,128)(2,1)}, u32[]{:S(2)}) copy-start(bf16[224,32]{0,1:T(8,128)(2,1)} %param.6) | copy-start | bytes 43012
  2.5 1.8 %copy-start.1 = (bf16[32,16,1024]{2,1,0:T(8,128)(2,1)S(1)}, bf16[32,16,1024]{2,1,0:T(8,128)(2,1)}, u32[]{:S(2)}) copy-start(bf16[32,16,1024]{2,1,0:T(8,128)(2,1)} %param.5) | copy-start | bytes 3145732
  4.3 1.5 %copy-start.2 = (bf16[256,2044]{1,0:T(8,128)(2,1)}, bf16[256,2044]{1,0:T(8,128)(2,1)S(1)}, u32[]{:S(2)}) copy-start(bf16[256,2044]{1,0:T(8,128)(2,1)S(1)} %reshape.88) | copy-start | bytes 3139588
  7.4 13.8 %all-to-all-start = ((bf16[16,2,4096]{2,1,0:T(2,128)(2,1)}), bf16[16,2,4096]{2,1,0:T(2,128)(2,1)S(1)}, u32[]{:S(2)}, u32[]{:S(2)}) async-start(bf16[16,2,4096]{2,1,0:T(2,128)(2,1)} %reshape.104), calls=%async_computation | async-start | bytes 524288 | tf_op jit(solution)/shard_map/all_to_all | solution.py:88
  14.0 15.8 %copy-start.5 = (bf16[128,764]{1,0:T(8,128)(2,1)}, bf16[128,764]{1,0:T(8,128)(2,1)S(1)}, u32[]{:S(2)}) copy-start(bf16[128,764]{1,0:T(8,128)(2,1)S(1)} %reshape.86) | copy-start | bytes 586756
  15.5 9.4 %copy-start.8 = (bf16[8,224]{1,0:T(8,128)(2,1)S(1)}, bf16[8,224]{1,0:T(8,128)(2,1)}, u32[]{:S(2)}) copy-start(bf16[8,224]{1,0:T(8,128)(2,1)} %param.7) | copy-start | bytes 10756
  21.3 13.7 %all-to-all-start.1 = ((bf16[16,2,7168]{2,1,0:T(2,128)(2,1)}), bf16[16,2,7168]{2,1,0:T(2,128)(2,1)S(1)}, u32[]{:S(2)}, u32[]{:S(2)}) async-start(bf16[16,2,7168]{2,1,0:T(2,128)(2,1)} %reshape.102), calls=%async_computation.1 | async-start | bytes 917504 | tf_op jit(solution)/shard_map/all_to_all | solution.py:90
  25.0 4.8 %copy-start.6 = (f32[8,32,1]{1,0,2:T(8,128)}, f32[8,32,1]{1,0,2:T(8,128)S(1)}, u32[]{:S(2)}) copy-start(f32[8,32,1]{1,0,2:T(8,128)S(1)} %convolution_bitcast_fusion.2) | copy-start | bytes 3076
  35.5 1.4 %copy-start.4 = (f32[32,16,64]{2,1,0:T(8,128)S(1)}, f32[32,16,64]{2,1,0:T(8,128)}, u32[]{:S(2)}) copy-start(f32[32,16,64]{2,1,0:T(8,128)} %get-tuple-element.19) | copy-start | bytes 393220
  36.3 10.6 %slice-start = ((bf16[128,764]{1,0:T(8,128)(2,1)}), bf16[128,256]{1,0:T(8,128)(2,1)S(1)}, s32[]{:S(2)}) async-start(bf16[128,764]{1,0:T(8,128)(2,1)} %copy-done.5), calls=%async_computation.4 | async-start | bytes 131072 | tf_op jit(solution)/shard_map/slice | solution.py:53
  37.1 18.2 %collective-permute-start.1 = (f32[32,16,96]{2,1,0:T(8,128)S(1)}, f32[32,16,96]{2,1,0:T(8,128)S(1)}, u32[]{:S(2)}, u32[]{:S(2)}) collective-permute-start(f32[32,16,96]{2,1,0:T(8,128)S(1)} %pad_maximum_fusion.1), channel_id=1, source_target_pairs={{16,0},{32,16},{48,32},{64,48},{80,64},{96,80},{112,96},{128,112},... | collective-permute-start | bytes 589832 | tf_op jit(solution)/shard_map/ppermute | solution.py:111
  44.7 17.8 %collective-permute-start = (f32[32,16,96]{2,1,0:T(8,128)S(1)}, f32[32,16,96]{2,1,0:T(8,128)S(1)}, u32[]{:S(2)}, u32[]{:S(2)}) collective-permute-start(f32[32,16,96]{2,1,0:T(8,128)S(1)} %pad_maximum_fusion), channel_id=1, source_target_pairs={{0,16},{16,32},{32,48},{48,64},{64,80},{80,96},{96,112},{112,128},... | collective-permute-start | bytes 589832 | tf_op jit(solution)/shard_map/ppermute | solution.py:110
  68.1 11.6 %all-to-all-start.2 = ((bf16[16,2,4096]{2,1,0:T(2,128)(2,1)}), bf16[16,2,4096]{2,1,0:T(2,128)(2,1)S(1)}, u32[]{:S(2)}, u32[]{:S(2)}) async-start(bf16[16,2,4096]{2,1,0:T(2,128)(2,1)} %reshape.106), calls=%async_computation.2 | async-start | bytes 524288 | tf_op jit(solution)/shard_map/all_to_all | solution.py:142
  72.5 14.2 %copy-start.3 = (bf16[8,16,1024]{2,0,1:T(8,128)(2,1)S(1)}, bf16[8,16,1024]{2,0,1:T(8,128)(2,1)}, u32[]{:S(2)}) copy-start(bf16[8,16,1024]{2,0,1:T(8,128)(2,1)} %fusion.8) | copy-start | bytes 786436
  72.5 14.2 %copy-start.7 = (f32[8,32,1]{1,0,2:T(8,128)S(1)}, f32[8,32,1]{1,0,2:T(8,128)}, u32[]{:S(2)}) copy-start(f32[8,32,1]{1,0,2:T(8,128)} %copy-done.6) | copy-start | bytes 3076
  82.4 14.4 %all-to-all-start.3 = ((bf16[16,2,7168]{2,1,0:T(2,128)(2,1)}), bf16[16,2,7168]{2,1,0:T(2,128)(2,1)}, u32[]{:S(2)}, u32[]{:S(2)}) async-start(bf16[16,2,7168]{2,1,0:T(2,128)(2,1)} %reshape.108), calls=%async_computation.3 | async-start | bytes 917504 | tf_op jit(solution)/shard_map/all_to_all | solution.py:146
where the time goes:
time: 101 us; the launch traced here: 100 us
  waiting for transfers between devices  34.4 us (34%)
  starting transfers between devices  26.7 us (26%)
  local copies, waits for them, and re-layouts  23.2 us (23%)
  matrix products  12.4 us (12%)
  between operations  1.83 us (2%)
  other arithmetic  1.81 us (2%)
    unnamed x30, local copies, waits for them, and re-layouts  13.6 us
    ppermute x1, waiting for transfers between devices, shards(): got_next = lax.ppermute(to_prev, 'tile', [(i + 1, i) for i in range(ends)])  8.2 us
    ppermute x1, starting transfers between devices, shards(): got_next = lax.ppermute(to_prev, 'tile', [(i + 1, i) for i in range(ends)])  7.49 us
    ppermute x1, waiting for transfers between devices, shards(): got_prev = lax.ppermute(to_next, 'tile', [(i, i + 1) for i in range(ends)])  7.23 us
    all_to_all x1, waiting for transfers between devices, shards(): lax.all_to_all(back_split, 'spec', split_axis=0, concat_axis=3, tiled=True)  7.21 us
    all_to_all x1, starting transfers between devices, shards(): lax.all_to_all(cols_done, 'spec', split_axis=0, concat_axis=3, tiled=True)  5.76 us
    all_to_all x1, waiting for transfers between devices, shards(): lax.all_to_all(cols_done, 'spec', split_axis=0, concat_axis=3, tiled=True)  4.31 us
    all_to_all x1, starting transfers between devices, shards(): lax.all_to_all(resid_split, 'spec', split_axis=0, concat_axis=2, tiled=True)  4.22 us
  transfers between devices with their start and end apart: 6, of which 6 were waited for; matrix products, arithmetic and copies ran while one was open for 18% of the time, Pallas kernels for 0%

commit v1 on v0

--- a/solution.py
+++ b/solution.py
@@ -87,7 +87,12 @@
     ).astype(bf16)
     tile_rows = lax.all_to_all(cols_done, "spec", split_axis=0, concat_axis=3, tiled=True)[0]
     obs_split = hyper_obs.reshape(group, coarse_rows, n_spec, chunk).transpose(2, 0, 3, 1)
-    obs_cols = lax.all_to_all(obs_split, "spec", split_axis=0, concat_axis=1, tiled=True)[0]
+    obs_cols = jnp.concatenate(
+        lax.all_to_all(
+            jnp.stack(jnp.split(obs_split, lax.axis_size("spec"), axis=0)), "spec", 0, 0
+        ),
+        axis=1,
+    )[0]
     resp_basis = jnp.dot(response.astype(f32), basis_wide, precision=highest)
     multi_pred = jnp.einsum("mq,qrc->mrc", resp_basis, latent.astype(f32), precision=highest)
     multi_resid = (multi_pred - multi_obs.astype(f32)).astype(bf16)

time: 101 us -> 103 us (1.020)
  other arithmetic: 1.81 us -> 3.47 us
    unnamed x30 -> x43, local copies, waits for them, and re-layouts: 13.6 us -> 13.8 us
  transfers between devices with their start and end apart: 6 -> 6, of which waited for: 6 -> 6; matrix products, arithmetic and copies ran while one was open for 18% -> 17% of each run, Pallas kernels for 0% -> 0%
where the time goes in v1:
time: 103 us; the launch traced here: 102 us
  waiting for transfers between devices  35.1 us (34%)
  starting transfers between devices  26.7 us (26%)
  local copies, waits for them, and re-layouts  23.3 us (23%)
  matrix products  11.7 us (11%)
  other arithmetic  3.47 us (3%)
  between operations  1.87 us (2%)
    unnamed x43, local copies, waits for them, and re-layouts  13.8 us
    ppermute x1, waiting for transfers between devices, shards(): got_prev = lax.ppermute(to_next, 'tile', [(i, i + 1) for i in range(ends)])  8.14 us
    ppermute x1, waiting for transfers between devices, shards(): got_next = lax.ppermute(to_prev, 'tile', [(i + 1, i) for i in range(ends)])  7.5 us
    ppermute x1, starting transfers between devices, shards(): got_next = lax.ppermute(to_prev, 'tile', [(i + 1, i) for i in range(ends)])  7.49 us
    all_to_all x1, waiting for transfers between devices, shards(): lax.all_to_all(back_split, 'spec', split_axis=0, concat_axis=3, tiled=True)  7.23 us
    all_to_all x1, starting transfers between devices, shards(): lax.all_to_all(cols_done, 'spec', split_axis=0, concat_axis=3, tiled=True)  5.76 us
    all_to_all x1, waiting for transfers between devices, shards(): lax.all_to_all(jnp.stack(jnp.split(obs_split, lax.axis_size('spec'), axis...  4.76 us
    all_to_all x1, starting transfers between devices, shards(): lax.all_to_all(resid_split, 'spec', split_axis=0, concat_axis=2, tiled=True)  4.22 us
  transfers between devices with their start and end apart: 6, of which 6 were waited for; matrix products, arithmetic and copies ran while one was open for 17% of the time, Pallas kernels for 0%

profile of v1, /device:TPU:24, one launch (start us, length us, event | category | flops | bytes accessed | tf_op | source)
XLA Modules:
  0.0 102.1 jit_solution(7778482799966785292)
XLA Ops:
  0.6 0.7 fusion.65
  2.0 0.2 broadcast_bitcast_fusion
  2.3 0.2 copy.89
  2.6 1.7 %reshape.84 = bf16[256,2044]{1,0:T(8,128)(2,1)S(1)} reshape(bf16[523264]{0:T(1024)(128)(2,1)S(1)} %slice.70) | data formatting | bytes 2093056 | tf_op jit(solution)/shard_map/reshape | solution.py:53
  4.3 1.4 %fusion.71 = bf16[16,16,16,32]{3,2,1,0:T(8,128)(2,1)S(1)} fusion(bf16[16,16,1024,1]{2,1,3,0:T(8,128)(2,1)S(1)} %bitcast.230, bf16[32,16,1024]{2,1,0:T(8,128)(2,1)S(1)} %copy-done.1), kind=kOutput, calls=%fused_computation.117 | convolution fusion | flops 268566528 | bytes 1835008 | tf_op jit(solution)/shard_map/qrc,sjc->sqjr/dot_general | solution.py:82
  5.8 1.7 %reshape.100 = bf16[16,2,4096]{2,1,0:T(2,128)(2,1)} reshape(bf16[16,16,16,32]{3,2,1,0:T(8,128)(2,1)S(1)} %fusion.71) | data formatting | bytes 524288
  7.4 5.8 %all-to-all-start = ((bf16[16,2,4096]{2,1,0:T(2,128)(2,1)}), bf16[16,2,4096]{2,1,0:T(2,128)(2,1)S(1)}, u32[]{:S(2)}, u32[]{:S(2)}) async-start(bf16[16,2,4096]{2,1,0:T(2,128)(2,1)} %reshape.100), calls=%async_computation | async-start | bytes 524288 | tf_op jit(solution)/shard_map/all_to_all | solution.py:88
  13.2 1.4 %copy.44 = bf16[14,64,256]{1,2,0:T(8,128)(2,1)S(1)} copy(bf16[14,64,256]{2,1,0:T(8,128)(2,1)} %param.8) | data formatting | bytes 917504 | tf_op args[3]
  15.0 1.3 %reshape.98 = bf16[16,2,7168]{2,1,0:T(2,128)(2,1)} reshape(bf16[16,1,14,16,64]{4,3,2,1,0:T(8,128)(2,1)S(1)} %fusion.27) | data formatting | bytes 917504
  16.6 0.5 reshape.82
  17.1 4.2 %all-to-all-done = bf16[16,2,4096]{2,1,0:T(2,128)(2,1)S(1)} async-done(((bf16[16,2,4096]{2,1,0:T(2,128)(2,1)}), bf16[16,2,4096]{2,1,0:T(2,128)(2,1)S(1)}, u32[]{:S(2)}, u32[]{:S(2)}) %all-to-all-start) | async-done | bytes 262176 | tf_op jit(solution)/shard_map/all_to_all | solution.py:88
  21.3 3.6 %all-to-all-start.1 = ((bf16[16,2,7168]{2,1,0:T(2,128)(2,1)}), bf16[16,2,7168]{2,1,0:T(2,128)(2,1)S(1)}, u32[]{:S(2)}, u32[]{:S(2)}) async-start(bf16[16,2,7168]{2,1,0:T(2,128)(2,1)} %reshape.98), calls=%async_computation.1 | async-start | bytes 917504 | tf_op jit(solution)/shard_map/all_to_all | solution.py:91
  25.0 2.5 %fusion.8 = bf16[8,16,1024]{2,0,1:T(8,128)(2,1)S(1)} fusion(f32[8,32,1]{1,0,2:T(8,128)S(1)} %convolution_bitcast_fusion.2, bf16[32,16,1024]{2,1,0:T(8,128)(2,1)S(1)} %copy-done.1, bf16[8,16,1024]{2,1,0:T(8,128)(2,1)} %param.9), kind=kOutput, calls=%fused_computation.13 | convolution fusion | flops 50724864 | bytes 1573888 | tf_op jit(solution)/shard_map/mq,qrc->mrc/dot_general | solution.py:97
  27.5 0.5 reshape.101
  28.0 1.1 %copy.41 = bf16[32,16,256]{2,1,0:T(8,128)(2,1)S(1)} copy(bf16[32,16,256]{0,1,2:T(8,128)(2,1)S(1)} %bitcast.202) | data formatting | bytes 524288 | tf_op jit(solution)/shard_map/squeeze | solution.py:88
  29.1 0.2 fusion.25
  29.3 0.9 fusion.69
  30.2 4.8 %all-to-all-done.1 = bf16[16,2,7168]{2,1,0:T(2,128)(2,1)S(1)} async-done(((bf16[16,2,7168]{2,1,0:T(2,128)(2,1)}), bf16[16,2,7168]{2,1,0:T(2,128)(2,1)S(1)}, u32[]{:S(2)}, u32[]{:S(2)}) %all-to-all-start.1) | async-done | bytes 458784 | tf_op jit(solution)/shard_map/all_to_all | solution.py:91
  35.0 0.5 reshape.99
  35.5 0.7 copy.59
  36.3 0.3 fusion.46
  36.9 1.1 %pad_maximum_fusion.1 = f32[32,16,96]{2,1,0:T(8,128)S(1)} fusion(f32[32,16,32]{2,1,0:T(8,128)S(1)} %get-tuple-element.19, f32[32,16,64]{2,1,0:T(8,128)} %get-tuple-element.17), kind=kLoop, calls=%fused_computation.31 | loop fusion | flops 49152 | bytes 393216 | tf_op jit(solution)/shard_map/concatenate | solution.py:111
  38.0 7.5 %collective-permute-start.1 = (f32[32,16,96]{2,1,0:T(8,128)S(1)}, f32[32,16,96]{2,1,0:T(8,128)S(1)}, u32[]{:S(2)}, u32[]{:S(2)}) collective-permute-start(f32[32,16,96]{2,1,0:T(8,128)S(1)} %pad_maximum_fusion.1), channel_id=1, source_target_pairs={{16,0},{32,16},{48,32},{64,48},{80,64},{96,80},{112,96},{128,112},... | collective-permute-start | bytes 589832 | tf_op jit(solution)/shard_map/ppermute | solution.py:116
  45.5 0.8 pad_maximum_fusion
  46.4 2.1 %collective-permute-start = (f32[32,16,96]{2,1,0:T(8,128)}, f32[32,16,96]{2,1,0:T(8,128)S(1)}, u32[]{:S(2)}, u32[]{:S(2)}) collective-permute-start(f32[32,16,96]{2,1,0:T(8,128)} %pad_maximum_fusion), channel_id=1, source_target_pairs={{0,16},{16,32},{32,48},{48,64},{64,80},{80,96},{96,112},{112,128},... | collective-permute-start | bytes 589832 | tf_op jit(solution)/shard_map/ppermute | solution.py:115
  48.7 7.5 %collective-permute-done.1 = f32[32,16,96]{2,1,0:T(8,128)S(1)} collective-permute-done((f32[32,16,96]{2,1,0:T(8,128)S(1)}, f32[32,16,96]{2,1,0:T(8,128)S(1)}, u32[]{:S(2)}, u32[]{:S(2)}) %collective-permute-start.1) | collective-permute-done | bytes 196640 | tf_op jit(solution)/shard_map/ppermute | solution.py:116
  56.2 8.1 %collective-permute-done = f32[32,16,96]{2,1,0:T(8,128)S(1)} collective-permute-done((f32[32,16,96]{2,1,0:T(8,128)}, f32[32,16,96]{2,1,0:T(8,128)S(1)}, u32[]{:S(2)}, u32[]{:S(2)}) %collective-permute-start) | collective-permute-done | bytes 196640 | tf_op jit(solution)/shard_map/ppermute | solution.py:115
  64.8 0.3 fusion.23
  65.1 0.3 fusion.7
  65.5 0.3 convolution_bitcast_fusion
  66.0 0.4 fusion.15
  66.7 0.2 maximum_subtract_fusion
  67.2 0.5 fusion.20
  67.8 0.5 fusion.74
  68.3 1.7 %reshape.102 = bf16[16,2,4096]{2,1,0:T(2,128)(2,1)} reshape(bf16[16,16,16,32]{3,2,1,0:T(8,128)(2,1)S(1)} %fusion.74) | data formatting | bytes 524288
  70.0 3.5 %all-to-all-start.2 = ((bf16[16,2,4096]{2,1,0:T(2,128)(2,1)}), bf16[16,2,4096]{2,1,0:T(2,128)(2,1)S(1)}, u32[]{:S(2)}, u32[]{:S(2)}) async-start(bf16[16,2,4096]{2,1,0:T(2,128)(2,1)} %reshape.102), calls=%async_computation.2 | async-start | bytes 524288 | tf_op jit(solution)/shard_map/all_to_all | solution.py:147
  73.5 0.8 copy.70
  74.3 7.2 %all-to-all-done.2 = bf16[16,2,4096]{2,1,0:T(2,128)(2,1)S(1)} async-done(((bf16[16,2,4096]{2,1,0:T(2,128)(2,1)}), bf16[16,2,4096]{2,1,0:T(2,128)(2,1)S(1)}, u32[]{:S(2)}, u32[]{:S(2)}) %all-to-all-start.2) | async-done | bytes 262176 | tf_op jit(solution)/shard_map/all_to_all | solution.py:147
  81.6 1.5 %reshape.103 = bf16[16,16,16,32]{3,2,1,0:T(8,128)(2,1)} reshape(bf16[16,2,4096]{2,1,0:T(2,128)(2,1)S(1)} %all-to-all-done.2) | data formatting | bytes 524288
  83.0 1.3 %reshape.104 = bf16[16,2,7168]{2,1,0:T(2,128)(2,1)} reshape(bf16[16,14,16,64]{3,2,1,0:T(8,128)(2,1)S(1)} %bitcast.206) | data formatting | bytes 917504
  84.3 4.2 %all-to-all-start.3 = ((bf16[16,2,7168]{2,1,0:T(2,128)(2,1)}), bf16[16,2,7168]{2,1,0:T(2,128)(2,1)}, u32[]{:S(2)}, u32[]{:S(2)}) async-start(bf16[16,2,7168]{2,1,0:T(2,128)(2,1)} %reshape.104), calls=%async_computation.3 | async-start | bytes 917504 | tf_op jit(solution)/shard_map/all_to_all | solution.py:151
  88.5 1.0 fusion.77
  89.6 2.4 %copy.68 = bf16[32,16,256]{2,1,0:T(8,128)(2,1)S(1)} copy(bf16[32,16,256]{0,1,2:T(8,128)(2,1)} %bitcast.201) | data formatting | bytes 524288 | tf_op jit(solution)/shard_map/squeeze | solution.py:147
  92.0 3.4 %fusion.2 = bf16[32,16,1024]{2,1,0:T(8,128)(2,1)} fusion(f32[32,16,1024]{2,0,1:T(8,128)S(1)} %fusion.77, bf16[32,16,1024]{2,1,0:T(8,128)(2,1)S(1)} %copy-done.1, bf16[32,16,256]{2,1,0:T(8,128)(2,1)S(1)} %copy.68, bf16[256,2044]{1,0:T(8,128)(2,1)} %copy-done.2), kind=kOutput, calls=%fused_computation.3 | convolution fusion | flops 271056896 | bytes 4980736 | tf_op jit(solution)/shard_map/qrj,jc->qrc/dot_general | solution.py:148
  95.4 3.3 %all-to-all-done.3 = bf16[16,2,7168]{2,1,0:T(2,128)(2,1)} async-done(((bf16[16,2,7168]{2,1,0:T(2,128)(2,1)}), bf16[16,2,7168]{2,1,0:T(2,128)(2,1)}, u32[]{:S(2)}, u32[]{:S(2)}) %all-to-all-start.3) | async-done | bytes 458784 | tf_op jit(solution)/shard_map/all_to_all | solution.py:151
  98.7 2.1 %reshape.105 = bf16[16,14,16,64]{3,2,1,0:T(8,128)(2,1)S(1)} reshape(bf16[16,2,7168]{2,1,0:T(2,128)(2,1)} %all-to-all-done.3) | data formatting | bytes 917504
  100.8 0.2 copy.71
  101.0 1.1 %copy.72 = bf16[14,64,256]{2,1,0:T(8,128)(2,1)} copy(bf16[14,64,256]{1,2,0:T(8,128)(2,1)S(1)} %bitcast.205) | data formatting | bytes 917504
  (54 shorter events, 2.5 us)
Async XLA Ops:
  0.6 24.2 %copy-start = (bf16[224,32]{0,1:T(8,128)(2,1)S(1)}, bf16[224,32]{0,1:T(8,128)(2,1)}, u32[]{:S(2)}) copy-start(bf16[224,32]{0,1:T(8,128)(2,1)} %param.6) | copy-start | bytes 43012
  2.5 1.8 %copy-start.1 = (bf16[32,16,1024]{2,1,0:T(8,128)(2,1)S(1)}, bf16[32,16,1024]{2,1,0:T(8,128)(2,1)}, u32[]{:S(2)}) copy-start(bf16[32,16,1024]{2,1,0:T(8,128)(2,1)} %param.5) | copy-start | bytes 3145732
  4.3 1.5 %copy-start.2 = (bf16[256,2044]{1,0:T(8,128)(2,1)}, bf16[256,2044]{1,0:T(8,128)(2,1)S(1)}, u32[]{:S(2)}) copy-start(bf16[256,2044]{1,0:T(8,128)(2,1)S(1)} %reshape.84) | copy-start | bytes 3139588
  7.4 13.8 %all-to-all-start = ((bf16[16,2,4096]{2,1,0:T(2,128)(2,1)}), bf16[16,2,4096]{2,1,0:T(2,128)(2,1)S(1)}, u32[]{:S(2)}, u32[]{:S(2)}) async-start(bf16[16,2,4096]{2,1,0:T(2,128)(2,1)} %reshape.100), calls=%async_computation | async-start | bytes 524288 | tf_op jit(solution)/shard_map/all_to_all | solution.py:88
  14.8 10.0 %copy-start.7 = (bf16[8,224]{1,0:T(8,128)(2,1)S(1)}, bf16[8,224]{1,0:T(8,128)(2,1)}, u32[]{:S(2)}) copy-start(bf16[8,224]{1,0:T(8,128)(2,1)} %param.7) | copy-start | bytes 10756
  17.1 13.1 %copy-start.6 = (bf16[128,764]{1,0:T(8,128)(2,1)}, bf16[128,764]{1,0:T(8,128)(2,1)S(1)}, u32[]{:S(2)}) copy-start(bf16[128,764]{1,0:T(8,128)(2,1)S(1)} %reshape.82) | copy-start | bytes 586756
  21.3 13.7 %all-to-all-start.1 = ((bf16[16,2,7168]{2,1,0:T(2,128)(2,1)}), bf16[16,2,7168]{2,1,0:T(2,128)(2,1)S(1)}, u32[]{:S(2)}, u32[]{:S(2)}) async-start(bf16[16,2,7168]{2,1,0:T(2,128)(2,1)} %reshape.98), calls=%async_computation.1 | async-start | bytes 917504 | tf_op jit(solution)/shard_map/all_to_all | solution.py:91
  35.5 10.0 %copy-start.3 = (f32[32,16,64]{2,1,0:T(8,128)S(1)}, f32[32,16,64]{2,1,0:T(8,128)}, u32[]{:S(2)}) copy-start(f32[32,16,64]{2,1,0:T(8,128)} %get-tuple-element.16) | copy-start | bytes 393220
  36.3 12.2 %slice-start = ((bf16[128,764]{1,0:T(8,128)(2,1)}), bf16[128,256]{1,0:T(8,128)(2,1)S(1)}, s32[]{:S(2)}) async-start(bf16[128,764]{1,0:T(8,128)(2,1)} %copy-done.6), calls=%async_computation.4 | async-start | bytes 131072 | tf_op jit(solution)/shard_map/slice | solution.py:53
  38.0 18.2 %collective-permute-start.1 = (f32[32,16,96]{2,1,0:T(8,128)S(1)}, f32[32,16,96]{2,1,0:T(8,128)S(1)}, u32[]{:S(2)}, u32[]{:S(2)}) collective-permute-start(f32[32,16,96]{2,1,0:T(8,128)S(1)} %pad_maximum_fusion.1), channel_id=1, source_target_pairs={{16,0},{32,16},{48,32},{64,48},{80,64},{96,80},{112,96},{128,112},... | collective-permute-start | bytes 589832 | tf_op jit(solution)/shard_map/ppermute | solution.py:116
  46.4 18.0 %collective-permute-start = (f32[32,16,96]{2,1,0:T(8,128)}, f32[32,16,96]{2,1,0:T(8,128)S(1)}, u32[]{:S(2)}, u32[]{:S(2)}) collective-permute-start(f32[32,16,96]{2,1,0:T(8,128)} %pad_maximum_fusion), channel_id=1, source_target_pairs={{0,16},{16,32},{32,48},{48,64},{64,80},{80,96},{96,112},{112,128},... | collective-permute-start | bytes 589832 | tf_op jit(solution)/shard_map/ppermute | solution.py:115
  56.2 8.3 %copy-start.4 = (f32[32,16,96]{2,1,0:T(8,128)}, f32[32,16,96]{2,1,0:T(8,128)S(1)}, u32[]{:S(2)}) copy-start(f32[32,16,96]{2,1,0:T(8,128)S(1)} %collective-permute-done.1) | copy-start | bytes 589828
  65.1 1.4 %copy-start.5 = (f32[32,16,96]{2,1,0:T(8,128)S(1)}, f32[32,16,96]{2,1,0:T(8,128)}, u32[]{:S(2)}) copy-start(f32[32,16,96]{2,1,0:T(8,128)} %copy-done.4) | copy-start | bytes 589828
  70.0 11.6 %all-to-all-start.2 = ((bf16[16,2,4096]{2,1,0:T(2,128)(2,1)}), bf16[16,2,4096]{2,1,0:T(2,128)(2,1)S(1)}, u32[]{:S(2)}, u32[]{:S(2)}) async-start(bf16[16,2,4096]{2,1,0:T(2,128)(2,1)} %reshape.102), calls=%async_computation.2 | async-start | bytes 524288 | tf_op jit(solution)/shard_map/all_to_all | solution.py:147
  84.3 14.4 %all-to-all-start.3 = ((bf16[16,2,7168]{2,1,0:T(2,128)(2,1)}), bf16[16,2,7168]{2,1,0:T(2,128)(2,1)}, u32[]{:S(2)}, u32[]{:S(2)}) async-start(bf16[16,2,7168]{2,1,0:T(2,128)(2,1)} %reshape.104), calls=%async_computation.3 | async-start | bytes 917504 | tf_op jit(solution)/shard_map/all_to_all | solution.py:151
